TPU v7x, 32 devices: a whole 2x2x4 slice. The times are simulated.
32 devices in a mesh: px: 4 (over y, x), py: 8 (over z, core).
Axes of the slice: x: 2, y: 2, z: 4, core: 2. Of those that a mesh axis runs over, the one named last changes fastest.
Arguments:
- residual: float32 [10, 2048, 2048], P(None, 'py', 'px'), may hold values from -6 to 6
- lambda_x: float32 [2048], P('px'), may hold values from 0.1 to 4
- lambda_y: float32 [2048], P('py'), may hold values from 0.1 to 4
- coupling: float32 [9], replicated, may hold values from 0.2 to 2
- layer_shift: float32 [10], replicated, may hold values from 0.05 to 1
- left_x: bfloat16 [2048, 2048], P(None, 'px'), may hold values from -0.125 to 0.125
- left_y: bfloat16 [2048, 2048], P('py'), may hold values from -0.125 to 0.125
- right_y: bfloat16 [2048, 2048], P('py'), may hold values from -0.125 to 0.125
- right_x: bfloat16 [2048, 2048], P(None, 'px'), may hold values from -0.125 to 0.125
- regime_code: int32 [10, 2048, 2048], P(None, 'py', 'px'), may hold values from 0 to 3
- upwind_flag: int32 [2, 10, 2048, 2048], P(None, None, 'py', 'px'), may hold values from 0 to 1
- mobility_table: float32 [4], replicated, may hold values from 0.3 to 3
Outputs:
- correction: float32 [10, 2048, 2048], P(None, 'py', 'px')
- balance: float32 [10, 2048, 2048], P(None, 'py', 'px')
Inputs may be any that keep to these rules, and one draw needn't show every extreme that they name: `regime_code`: a regime number of each cell.
All inputs are finite; a program needn't handle non-finite values.
Results may differ from a plain program's by a relative error of at most 0.0057.
Values may be sent and summed in bfloat16 or wider, within the bound.
No kernel may reach another device: no remote copies, remote signals or barrier semaphores. Data moves between devices by JAX's collectives and lax.ppermute only.
A program may use at most 192 MiB of HBM per device.

v0:
```python
import jax
import jax.numpy as jnp
from jax import lax
from jax.sharding import PartitionSpec as P


def with_halo(block, sides, width):
    for axis, dim in sides:
        count = lax.axis_size(axis)
        forward = [(i, i + 1) for i in range(count - 1)]
        backward = [(target, source) for source, target in forward]
        low = lax.ppermute(
            lax.slice_in_dim(block, block.shape[dim] - width, None, axis=dim), axis, forward
        )
        high = lax.ppermute(lax.slice_in_dim(block, 0, width, axis=dim), axis, backward)
        block = jnp.concatenate([low, block, high], axis=dim)
    return block


def thomas_solve(rhs, lambda_x, lambda_y, coupling, layer_shift):
    layers = rhs.shape[0]
    mode_sum = lambda_y[:, None] + lambda_x[None, :]
    ratios = []
    partial_values = []
    for layer_index in range(layers):
        diagonal = mode_sum + layer_shift[layer_index]
        if layer_index > 0:
            diagonal = diagonal + coupling[layer_index - 1]
        if layer_index < layers - 1:
            diagonal = diagonal + coupling[layer_index]
        if layer_index == 0:
            pivots = diagonal
            solved = rhs[0] / pivots
        else:
            pivots = diagonal + coupling[layer_index - 1] * ratios[-1]
            solved = (rhs[layer_index] + coupling[layer_index - 1] * partial_values[-1]) / pivots
        partial_values.append(solved)
        if layer_index < layers - 1:
            ratios.append(-coupling[layer_index] / pivots)
    results = [partial_values[layers - 1]]
    for layer_index in range(layers - 2, -1, -1):
        results.append(partial_values[layer_index] - ratios[layer_index] * results[-1])
    return jnp.stack(results[::-1])


def shards(
    residual,
    lambda_x,
    lambda_y,
    coupling,
    layer_shift,
    left_x,
    left_y,
    right_y,
    right_x,
    regime_code,
    upwind_flag,
    mobility_table,
):
    rounded = residual.astype(jnp.bfloat16)

    def forward(block):
        weights = left_x
        spectral_x = jnp.einsum(
            "zyx,xi->zyi",
            lax.all_gather(block, "px", axis=2, tiled=True),
            weights,
            preferred_element_type=jnp.float32,
        ).astype(jnp.bfloat16)
        weights = left_y
        return jnp.einsum(
            "jy,zyi->zji",
            weights,
            lax.all_gather(spectral_x, "py", axis=1, tiled=True),
            preferred_element_type=jnp.float32,
        )

    mobility = jnp.zeros(regime_code.shape, jnp.float32)
    for regime in range(mobility_table.shape[0]):
        mobility = jnp.where(regime_code == regime, mobility_table[regime], mobility)
    spectral = forward(rounded)
    solved = thomas_solve(spectral, lambda_x, lambda_y, coupling, layer_shift).astype(jnp.bfloat16)
    weights = right_y
    back_y = jnp.einsum(
        "yj,zji->zyi",
        weights,
        lax.all_gather(solved, "py", axis=1, tiled=True),
        preferred_element_type=jnp.float32,
    ).astype(jnp.bfloat16)
    weights = right_x
    correction = jnp.einsum(
        "zyi,ix->zyx",
        lax.all_gather(back_y, "px", axis=2, tiled=True),
        weights,
        preferred_element_type=jnp.float32,
    )
    width_x = correction.shape[2]
    width_y = correction.shape[1]
    stacked = jnp.stack(
        [
            correction,
            mobility,
            upwind_flag[0].astype(jnp.float32),
            upwind_flag[1].astype(jnp.float32),
        ]
    )
    extended = with_halo(stacked, (("px", 3), ("py", 2)), 1)
    press_x = extended[0][:, 1:-1, :]
    mobil_x = extended[1][:, 1:-1, :]
    flags_x = extended[2][:, 1:-1, :]
    upwind_x = jnp.where(flags_x[:, :, :-1] > 0.5, mobil_x[:, :, :-1], mobil_x[:, :, 1:])
    flux_x = upwind_x * (press_x[:, :, :-1] - press_x[:, :, 1:])
    faces_x = lax.axis_index("px") * width_x + jnp.arange(width_x + 1, dtype=jnp.int32)
    valid_x = (faces_x >= 1) & (faces_x <= width_x * lax.axis_size("px") - 1)
    flux_x = jnp.where(valid_x[None, None, :], flux_x, 0.0)
    net_x = flux_x[:, :, 1:] - flux_x[:, :, :-1]
    press_y = extended[0][:, :, 1:-1]
    mobil_y = extended[1][:, :, 1:-1]
    flags_y = extended[3][:, :, 1:-1]
    upwind_y = jnp.where(flags_y[:, :-1, :] > 0.5, mobil_y[:, :-1, :], mobil_y[:, 1:, :])
    flux_y = upwind_y * (press_y[:, :-1, :] - press_y[:, 1:, :])
    faces_y = lax.axis_index("py") * width_y + jnp.arange(width_y + 1, dtype=jnp.int32)
    valid_y = (faces_y >= 1) & (faces_y <= width_y * lax.axis_size("py") - 1)
    flux_y = jnp.where(valid_y[None, :, None], flux_y, 0.0)
    net_y = flux_y[:, 1:, :] - flux_y[:, :-1, :]
    balance = net_x + net_y
    return (correction, balance)


def solution(mesh):
    return jax.shard_map(
        shards,
        mesh=mesh,
        in_specs=(
            P(None, "py", "px"),
            P("px"),
            P("py"),
            P(),
            P(),
            P(None, "px"),
            P("py", None),
            P("py", None),
            P(None, "px"),
            P(None, "py", "px"),
            P(None, None, "py", "px"),
            P(),
        ),
        out_specs=(P(None, "py", "px"), P(None, "py", "px")),
        check_vma=False,
    )
```

profile of v0, /device:TPU:3, one launch (start us, length us, event | category | flops | bytes accessed | tf_op | source)
XLA Modules:
  0.0 841.1 jit_solution(6633718282841774213)
XLA Ops:
  7.2 4.5 convert_element_type.21
  11.8 106.2 %all-gather.5.cloned.1.call-done = bf16[10,256,2048]{2,1,0:T(8,128)(2,1)} async-done(((bf16[10,256,512]{2,1,0:T(8,128)(2,1)}), bf16[10,256,2048]{2,1,0:T(8,128)(2,1)}) %all-gather.5.cloned.1.call-update) | async-done | bytes 10485776 | tf_op jit(solution)/shard_map/all_gather | solution.py:66
  118.0 9.4 %fusion.9 = bf16[10,256,512]{1,2,0:T(8,128)(2,1)} fusion(bf16[10,256,2048]{2,1,0:T(8,128)(2,1)} %all-gather.5.cloned.1.call-done, bf16[2048,512]{1,0:T(8,128)(2,1)S(1)} %copy-done), kind=kOutput, calls=%fused_computation.41 | convolution fusion | flops 5370019840 | bytes 15204352 | tf_op jit(solution)/shard_map/zyx,xi->zyi/dot_general | solution.py:64
  134.9 179.7 %all-gather.7.cloned.1.call-done = bf16[10,2048,512]{1,2,0:T(8,128)(2,1)} async-done(((bf16[10,256,512]{1,2,0:T(8,128)(2,1)}), bf16[10,2048,512]{1,2,0:T(8,128)(2,1)}) %all-gather.7.cloned.1.call-update) | async-done | bytes 20971536 | tf_op jit(solution)/shard_map/all_gather | solution.py:74
  314.6 10.3 %convolution_bitcast_fusion = f32[10,256,512]{1,2,0:T(8,128)S(1)} fusion(bf16[10,2048,512]{1,2,0:T(8,128)(2,1)} %all-gather.7.cloned.1.call-done, bf16[256,2048]{1,0:T(8,128)(2,1)S(1)} %copy-done.16), kind=kOutput, calls=%fused_computation.36 | convolution fusion | flops 5368709120 | bytes 27262976 | tf_op jit(solution)/shard_map/jy,zyi->zji/dot_general | solution.py:71
  324.9 14.8 %fusion.59 = (bf16[10,256,512]{1,2,0:T(8,128)(2,1)}, bf16[1,256,512]{1,2,0:T(8,128)(2,1)S(1)}, f32[1,256,512]{1,2,0:T(8,128)S(1)}, f32[1,256,512]{1,2,0:T(8,128)...) fusion(f32[]{:T(128)S(6)} %neg.27, f32[]{:T(128)} %bitcast.4, ...), kind=kLoop, calls=%fused_computation.107 | loop fusion | flops 13631487 | bytes 8916080
  340.4 4.8 convert_dynamic-update-slice_fusion.7
  345.9 7.5 convert_dynamic-update-slice_fusion.5
  354.1 10.2 %convert_dynamic-update-slice_fusion.3 = bf16[10,256,512]{1,2,0:T(8,128)(2,1)} fusion(bf16[10,256,512]{1,2,0:T(8,128)(2,1)} %convert_dynamic-update-slice_fusion.4, f32[1,256,512]{1,2,0:T(8,128)S(1)} %get-tuple-element.7, f32[1,256,512]{1,2,0:T(8,128)S(1)} %get-tuple-element.6, f32[]{:T(128)} %bitcast.3, f32[]{:T(128)S(6)} %neg.27, f32[]{:T(128)} %bitcast.4, ...), kind=kLoop, calls=%fused_computation.111 | loop fusion | flops 5636096 | bytes 1320988
  365.1 13.9 %convert_dynamic-update-slice_fusion.1 = bf16[10,256,512]{1,2,0:T(8,128)(2,1)} fusion(bf16[10,256,512]{1,2,0:T(8,128)(2,1)} %convert_dynamic-update-slice_fusion.2, f32[]{:T(128)} %bitcast.3, f32[]{:T(128)S(6)} %neg.27, f32[]{:T(128)} %bitcast.4, f32[]{:T(128)} %bitcast.5, f32[]{:T(128)S(6)} %neg.28, f32[]{:T(128)} %bitcast.6, f32[]{:T(128)} %bitcast.7, ...), kind=kLoop, calls=%fused_computation.109 | loop fusion | flops 8912896 | bytes 2372132
  379.0 13.9 %convert_dynamic-update-slice_fusion = bf16[10,256,512]{1,2,0:T(8,128)(2,1)} fusion(bf16[10,256,512]{1,2,0:T(8,128)(2,1)} %convert_dynamic-update-slice_fusion.1, f32[]{:T(128)} %bitcast.3, f32[]{:T(128)S(6)} %neg.27, f32[]{:T(128)} %bitcast.4, f32[]{:T(128)} %bitcast.5, f32[]{:T(128)S(6)} %neg.28, f32[]{:T(128)} %bitcast.6, f32[]{:T(128)} %bitcast.7, ...), kind=kLoop, calls=%fused_computation.108 | loop fusion | flops 8650752 | bytes 2372132 | tf_op jit(solution)/shard_map/stack | solution.py:43
  393.1 184.6 %all-gather.9.cloned.1.call-done = bf16[10,2048,512]{1,2,0:T(8,128)(2,1)} async-done(((bf16[10,256,512]{1,2,0:T(8,128)(2,1)}), bf16[10,2048,512]{1,2,0:T(8,128)(2,1)}) %all-gather.9.cloned.1.call-update) | async-done | bytes 20971536 | tf_op jit(solution)/shard_map/all_gather | solution.py:87
  577.7 22.0 %convert_bitcast_fusion = bf16[10,256,512]{2,1,0:T(8,128)(2,1)} fusion(bf16[10,2048,512]{1,2,0:T(8,128)(2,1)} %all-gather.9.cloned.1.call-done, bf16[256,2048]{1,0:T(8,128)(2,1)S(1)} %copy-done.17), kind=kOutput, calls=%fused_computation.25 | convolution fusion | flops 5370019840 | bytes 24641536 | tf_op jit(solution)/shard_map/yj,zji->zyi/dot_general | solution.py:84
  600.5 9.1 %select_bitcast_fusion = f32[1,10,256,512]{3,2,1,0:T(8,128)} fusion(s32[10,256,512]{2,1,0:T(8,128)} %param.21, f32[]{:T(128)} %bitcast.29, f32[]{:T(128)} %bitcast.28, f32[]{:T(128)} %bitcast.27, f32[]{:T(128)} %bitcast.26), kind=kLoop, calls=%fused_computation.24 | loop fusion | flops 10485760 | bytes 10485776 | tf_op jit(solution)/shard_map/stack | solution.py:99
  609.6 10.4 %slice_convert_fusion.1 = (f32[1,10,256,512]{3,2,1,0:T(8,128)}, f32[1,10,256,512]{3,2,1,0:T(8,128)}) fusion(s32[2,10,256,512]{3,2,1,0:T(8,128)} %param.22), kind=kLoop, calls=%fused_computation.23 | loop fusion | flops 2621440 | bytes 20971520 | tf_op jit(solution)/shard_map/convert_element_type | solution.py:103
  620.0 82.6 %all-gather.11.cloned.1.call-done = bf16[10,256,2048]{2,1,0:T(8,128)(2,1)} async-done(((bf16[10,256,512]{2,1,0:T(8,128)(2,1)}), bf16[10,256,2048]{2,1,0:T(8,128)(2,1)}) %all-gather.11.cloned.1.call-update) | async-done | bytes 10485776 | tf_op jit(solution)/shard_map/all_gather | solution.py:93
  702.6 8.5 %fusion.5 = f32[10,256,512]{2,1,0:T(8,128)S(1)} fusion(bf16[10,256,2048]{2,1,0:T(8,128)(2,1)} %all-gather.11.cloned.1.call-done, bf16[2048,512]{1,0:T(8,128)(2,1)S(1)} %copy-done.15), kind=kOutput, calls=%fused_computation.37 | convolution fusion | flops 5368709120 | bytes 17825792 | tf_op jit(solution)/shard_map/zyi,ix->zyx/dot_general | solution.py:91
  711.2 5.9 pad_maximum_fusion.4
  737.9 5.4 collective-permute-start.2
  749.3 27.6 %pad_maximum_fusion = f32[4,10,258,514]{3,2,1,0:T(8,128)} fusion(f32[4,10,1,514]{3,2,1,0:T(1,128)S(1)} %collective-permute-done.3, f32[4,10,256,1]{3,2,1,0:T(8,128)S(1)} %copy-done.8, f32[1,10,256,512]{3,2,1,0:T(8,128)} %get-tuple-element.19, f32[1,10,256,512]{3,2,1,0:T(8,128)S(1)} %bitcast.57, f32[1,10,256,512]{3,2,1,0:T(8,128)} %select_bitcast_fusion, ...), kind=kLoop, calls=%fused_computation | loop fusion | flops 37131360 | bytes 42435840 | tf_op jit(solution)/shard_map/concatenate | solution.py:16
  776.9 18.6 %slice_bitcast_fusion.3 = (f32[10,258,514]{2,1,0:T(8,128)}, f32[10,258,514]{2,1,0:T(8,128)}, f32[10,258,514]{2,1,0:T(8,128)}, f32[10,258,514]{2,1,0:T(8,128)}) fusion(f32[4,10,258,514]{3,2,1,0:T(8,128)} %pad_maximum_fusion), kind=kLoop, calls=%fused_computation.4 | loop fusion | bytes 42435840 | tf_op jit(solution)/shard_map/squeeze | solution.py:110
  795.5 14.9 %fusion.1 = f32[10,256,513]{2,1,0:T(8,128)} fusion(f32[10,258,514]{2,1,0:T(8,128)} %get-tuple-element.14, f32[10,258,514]{2,1,0:T(8,128)} %get-tuple-element.15, f32[10,258,514]{2,1,0:T(8,128)} %get-tuple-element.12, pred[513]{0:T(1024)(128)(4,1)S(1)} %fusion.62), kind=kLoop, calls=%fused_computation.7 | loop fusion | flops 6566400 | bytes 31519232 | tf_op jit(solution)/shard_map/jit(_where)/select_n | solution.py:115
  812.3 10.7 %fusion.3 = f32[10,257,512]{2,1,0:T(8,128)} fusion(f32[10,258,514]{2,1,0:T(8,128)S(1)} %copy-done.2, f32[10,258,514]{2,1,0:T(8,128)S(1)} %copy-done.3, f32[10,258,514]{2,1,0:T(8,128)} %get-tuple-element.13, pred[257]{0:T(512)(128)(4,1)S(1)} %fusion.65), kind=kLoop, calls=%fused_computation.12 | loop fusion | flops 6579200 | bytes 31580416 | tf_op jit(solution)/shard_map/jit(_where)/select_n | solution.py:124
  823.1 11.2 %fusion.4 = f32[10,256,512]{2,1,0:T(8,128)} fusion(f32[10,257,512]{2,1,0:T(8,128)} %fusion.3, f32[10,256,513]{2,1,0:T(8,128)} %fusion.1), kind=kLoop, calls=%fused_computation.16 | loop fusion | flops 3932160 | bytes 26214400 | tf_op jit(solution)/shard_map/add | solution.py:126
  (70 shorter events, 34.6 us)
Async XLA Ops:
  7.2 110.8 %copy-start = (bf16[2048,512]{1,0:T(8,128)(2,1)S(1)}, bf16[2048,512]{1,0:T(8,128)(2,1)}, u32[]{:S(2)}) copy-start(bf16[2048,512]{1,0:T(8,128)(2,1)} %param.17) | copy-start | bytes 6291460
  7.2 110.8 %all-gather.5.cloned.1.call-start = ((), (), s32[]{:S(2)}) async-start(), calls=%async_computation | async-start | bytes 13107200 | tf_op jit(solution)/shard_map/all_gather | solution.py:66
  11.7 116.3 %copy-start.12 = (f32[9]{0:T(128)S(1)}, f32[9]{0:T(128)}, u32[]{:S(2)}) copy-start(f32[9]{0:T(128)} %param.15) | copy-start | bytes 112
  11.7 122.4 %copy-start.11 = (f32[10]{0:T(128)S(1)}, f32[10]{0:T(128)}, u32[]{:S(2)}) copy-start(f32[10]{0:T(128)} %param.16) | copy-start | bytes 124
  11.8 302.8 %copy-start.16 = (bf16[256,2048]{1,0:T(8,128)(2,1)S(1)}, bf16[256,2048]{1,0:T(8,128)(2,1)}, u32[]{:S(2)}) copy-start(bf16[256,2048]{1,0:T(8,128)(2,1)} %param.18) | copy-start | bytes 3145732
  11.8 302.8 %all-gather.7.cloned.1.call-start = ((), (), s32[]{:S(2)}) async-start(), calls=%async_computation.1 | async-start | bytes 23592960 | tf_op jit(solution)/shard_map/all_gather | solution.py:74
  127.5 450.3 %all-gather.9.cloned.1.call-start = ((), (), s32[]{:S(2)}) async-start(), calls=%async_computation.2 | async-start | bytes 23592960 | tf_op jit(solution)/shard_map/all_gather | solution.py:87
  134.9 190.0 %copy-start.10 = (f32[512]{0:T(512)S(1)}, f32[512]{0:T(512)}, u32[]{:S(2)}) copy-start(f32[512]{0:T(512)} %param.13) | copy-start | bytes 6148
  134.9 190.0 %copy-start.13 = (f32[256]{0:T(256)S(1)}, f32[256]{0:T(256)}, u32[]{:S(2)}) copy-start(f32[256]{0:T(256)} %param.14) | copy-start | bytes 3076
  353.4 224.4 %copy-start.17 = (bf16[256,2048]{1,0:T(8,128)(2,1)S(1)}, bf16[256,2048]{1,0:T(8,128)(2,1)}, u32[]{:S(2)}) copy-start(bf16[256,2048]{1,0:T(8,128)(2,1)} %param.19) | copy-start | bytes 3145732
  392.9 206.9 %copy-start.14 = (f32[4]{0:T(128)S(1)}, f32[4]{0:T(128)}, u32[]{:S(2)}) copy-start(f32[4]{0:T(128)} %param.23) | copy-start | bytes 52
  392.9 309.7 %all-gather.11.cloned.1.call-start = ((), (), s32[]{:S(2)}) async-start(), calls=%async_computation.3 | async-start | bytes 13107200 | tf_op jit(solution)/shard_map/all_gather | solution.py:93
  609.6 93.0 %copy-start.15 = (bf16[2048,512]{1,0:T(8,128)(2,1)S(1)}, bf16[2048,512]{1,0:T(8,128)(2,1)}, u32[]{:S(2)}) copy-start(bf16[2048,512]{1,0:T(8,128)(2,1)} %param.20) | copy-start | bytes 6291460
  720.4 8.6 %collective-permute-start = (f32[4,10,256,1]{2,0,3,1:T(4,128)S(1)}, f32[4,10,256,1]{2,0,3,1:T(4,128)S(1)}, u32[]{:S(2)}, u32[]{:S(2)}) collective-permute-start(f32[4,10,256,1]{2,0,3,1:T(4,128)S(1)} %copy.14), channel_id=1, source_target_pairs={{0,8},{8,16},{16,24},{1,9},{9,17},{17,25},{2,10},{10,18},{18,26},{... | collective-permute-start | bytes 122888 | tf_op jit(solution)/shard_map/ppermute | solution.py:12
  726.8 5.6 collective-permute-start.1
  732.5 16.8 %slice-start = ((s8[5242880]{0:T(1024)(128)(4,1)}), s8[1048576]{0:T(1024)(128)(4,1)S(1)}, s32[]{:S(2)}) async-start(s8[5242880]{0:T(1024)(128)(4,1)} %bitcast.56), calls=%async_computation.4 | async-start | bytes 2097152
  735.6 13.7 %slice-start.1 = ((s8[5242880]{0:T(1024)(128)(4,1)}), s8[4194304]{0:T(1024)(128)(4,1)S(1)}, s32[]{:S(2)}) async-start(s8[5242880]{0:T(1024)(128)(4,1)} %bitcast.56), calls=%async_computation.5 | async-start | bytes 8388608
  735.6 13.7 %copy-start.7 = (f32[4,10,256,1]{3,2,1,0:T(8,128)S(1)}, f32[4,10,256,1]{3,2,1,0:T(8,128)}, u32[]{:S(2)}) copy-start(f32[4,10,256,1]{3,2,1,0:T(8,128)} %copy.16) | copy-start | bytes 122884
  735.6 13.7 %copy-start.8 = (f32[4,10,256,1]{3,2,1,0:T(8,128)S(1)}, f32[4,10,256,1]{3,2,1,0:T(8,128)}, u32[]{:S(2)}) copy-start(f32[4,10,256,1]{3,2,1,0:T(8,128)} %copy.17) | copy-start | bytes 122884
  737.9 7.5 collective-permute-start.2
  743.3 6.0 collective-permute-start.3
  795.5 14.9 %copy-start.2 = (f32[10,258,514]{2,1,0:T(8,128)S(1)}, f32[10,258,514]{2,1,0:T(8,128)}, u32[]{:S(2)}) copy-start(f32[10,258,514]{2,1,0:T(8,128)} %get-tuple-element.14) | copy-start | bytes 15913444
  795.5 16.9 %copy-start.3 = (f32[10,258,514]{2,1,0:T(8,128)S(1)}, f32[10,258,514]{2,1,0:T(8,128)}, u32[]{:S(2)}) copy-start(f32[10,258,514]{2,1,0:T(8,128)} %get-tuple-element.15) | copy-start | bytes 15913444
  823.1 11.2 %copy-start.1 = (bf16[2048,512]{1,0:T(8,128)(2,1)S(1)}, bf16[2048,512]{1,0:T(8,128)(2,1)}, u32[]{:S(2)}) copy-start(bf16[2048,512]{1,0:T(8,128)(2,1)} %param.17) | copy-start | bytes 6291460
  (4 other events, 31.6 us)
Sparse Core Ops, SparseCore 0:
  11.9 106.1 all-gather.4
  127.6 186.9 all-gather.6
  393.0 184.6 all-gather.8
  599.9 102.6 all-gather.10
where the time goes:
time: 845 us; the launch traced here: 841 us
  waiting for transfers between devices  557 us (66%)
  other arithmetic  164 us (19%)
  matrix products  50.2 us (6%)
  local copies, waits for them, and re-layouts  36.2 us (4%)
  between operations  19.7 us (2%)
  starting transfers between devices  13.6 us (2%)
    all_gather x1, waiting for transfers between devices, shards(): lax.all_gather(solved, 'py', axis=1, tiled=True)  185 us
    all_gather x1, waiting for transfers between devices, forward(): lax.all_gather(spectral_x, 'py', axis=1, tiled=True)  180 us
    all_gather x1, waiting for transfers between devices, forward(): lax.all_gather(block, 'px', axis=2, tiled=True)  106 us
    all_gather x1, waiting for transfers between devices, shards(): lax.all_gather(back_y, 'px', axis=2, tiled=True)  82.6 us
    unnamed x9, other arithmetic  53.4 us
    concatenate x1, other arithmetic, with_halo(): block = jnp.concatenate([low, block, high], axis=dim)  27.6 us
    dot_general x1, matrix products, shards(): jnp.einsum('yj,zji->zyi', weights, lax.all_gather(solved, 'py', axis=1, t...  22 us
    squeeze x1, local copies, waits for them, and re-layouts, shards(): flags_x = extended[2][:, 1:-1, :]  18.6 us
  transfers between devices with their start and end apart: 8, of which 6 were waited for; matrix products, arithmetic and copies ran while one was open for 3% of the time, Pallas kernels for 0%

commit v1 on v0

--- a/solution.py
+++ b/solution.py
@@ -2,6 +2,17 @@
 import jax.numpy as jnp
 from jax import lax
 from jax.sharding import PartitionSpec as P
+
+
+def collect(x, axis, dim):
+    ways = lax.axis_size(axis)
+    pieces = [x]
+    for far in range(1, ways):
+        pieces.append(
+            lax.ppermute(pieces[far - 1], axis, [(d, (d - 1) % ways) for d in range(ways)])
+        )
+    line = jnp.concatenate(pieces, axis=dim)
+    return jnp.roll(line, lax.axis_index(axis) * x.shape[dim], axis=dim)
 
 
 def with_halo(block, sides, width):
@@ -62,10 +73,7 @@
     def forward(block):
         weights = left_x
         spectral_x = jnp.einsum(
-            "zyx,xi->zyi",
-            lax.all_gather(block, "px", axis=2, tiled=True),
-            weights,
-            preferred_element_type=jnp.float32,
+            "zyx,xi->zyi", collect(block, "px", 2), weights, preferred_element_type=jnp.float32
         ).astype(jnp.bfloat16)
         weights = left_y
         return jnp.einsum(

time: 845 us -> 935 us (1.11)
  waiting for transfers between devices: 557 us -> 621 us
  local copies, waits for them, and re-layouts: 36.2 us -> 59.9 us
    ppermute x0 -> x3, waiting for transfers between devices: none -> 167 us  [collect(): lax.ppermute(pieces[far - 1], axis, [(d, (d - 1) % ways) for d in range(w...]
    all_gather x1 -> x0, waiting for transfers between devices: 106 us -> none  [forward(): lax.all_gather(block, 'px', axis=2, tiled=True)]
    unnamed x41 -> x55, local copies, waits for them, and re-layouts: 2.82 us -> 23 us
    unnamed x9 -> x10, other arithmetic: 53.4 us -> 58.4 us
  transfers between devices with their start and end apart: 8 -> 10, of which waited for: 6 -> 8; matrix products, arithmetic and copies ran while one was open for 3% -> 4% of each run, Pallas kernels for 0% -> 0%
where the time goes in v1:
time: 935 us; the launch traced here: 930 us
  waiting for transfers between devices  621 us (66%)
  other arithmetic  165 us (18%)
  local copies, waits for them, and re-layouts  59.9 us (6%)
  matrix products  50.3 us (5%)
  between operations  19.8 us (2%)
  starting transfers between devices  13.5 us (1%)
    all_gather x1, waiting for transfers between devices, shards(): lax.all_gather(solved, 'py', axis=1, tiled=True)  185 us
    all_gather x1, waiting for transfers between devices, forward(): lax.all_gather(spectral_x, 'py', axis=1, tiled=True)  184 us
    ppermute x3, waiting for transfers between devices, collect(): lax.ppermute(pieces[far - 1], axis, [(d, (d - 1) % ways) for d in range(w...  167 us
    all_gather x1, waiting for transfers between devices, shards(): lax.all_gather(back_y, 'px', axis=2, tiled=True)  82.6 us
    unnamed x10, other arithmetic  58.4 us
    concatenate x1, other arithmetic, with_halo(): block = jnp.concatenate([low, block, high], axis=dim)  27.6 us
    unnamed x55, local copies, waits for them, and re-layouts  23 us
    dot_general x1, matrix products, shards(): jnp.einsum('yj,zji->zyi', weights, lax.all_gather(solved, 'py', axis=1, t...  22 us
  transfers between devices with their start and end apart: 10, of which 8 were waited for; matrix products, arithmetic and copies ran while one was open for 4% of the time, Pallas kernels for 0%

profile of v1, /device:TPU:3, one launch (start us, length us, event | category | flops | bytes accessed | tf_op | source)
XLA Modules:
  0.0 929.7 jit_solution(320999438387402668)
XLA Ops:
  13.3 58.6 %collective-permute-done = bf16[10,256,512]{2,1,0:T(8,128)(2,1)S(1)} collective-permute-done((bf16[10,256,512]{2,1,0:T(8,128)(2,1)S(1)}, bf16[10,256,512]{2,1,0:T(8,128)(2,1)S(1)}, u32[]{:S(2)}, u32[]{:S(2)}) %collective-permute-start) | collective-permute-done | bytes 2621472 | tf_op jit(solution)/shard_map/ppermute | solution.py:12
  73.4 57.8 %collective-permute-done.1 = bf16[10,256,512]{2,1,0:T(8,128)(2,1)} collective-permute-done((bf16[10,256,512]{2,1,0:T(8,128)(2,1)S(1)}, bf16[10,256,512]{2,1,0:T(8,128)(2,1)}, u32[]{:S(2)}, u32[]{:S(2)}) %collective-permute-start.1) | collective-permute-done | bytes 2621472 | tf_op jit(solution)/shard_map/ppermute | solution.py:12
  138.2 50.1 %collective-permute-done.2 = bf16[10,256,512]{2,1,0:T(8,128)(2,1)} collective-permute-done((bf16[10,256,512]{2,1,0:T(8,128)(2,1)}, bf16[10,256,512]{2,1,0:T(8,128)(2,1)}, u32[]{:S(2)}, u32[]{:S(2)}) %collective-permute-start.2) | collective-permute-done | bytes 2621472 | tf_op jit(solution)/shard_map/ppermute | solution.py:12
  202.0 9.5 %fusion.10 = bf16[10,256,512]{1,2,0:T(8,128)(2,1)} fusion(bf16[2048,512]{1,0:T(8,128)(2,1)S(1)} %copy-done, bf16[10,256,4096]{2,1,0:T(8,128)(2,1)} %constant_dynamic-update-slice_fusion, s32[]{:T(128)S(6)} %select_n.43), kind=kOutput, calls=%fused_computation.42 | convolution fusion | flops 5370019840 | bytes 15204356 | tf_op jit(solution)/shard_map/zyx,xi->zyi/dot_general | solution.py:75
  219.0 183.5 %all-gather.4.cloned.1.call-done = bf16[10,2048,512]{1,2,0:T(8,128)(2,1)} async-done(((bf16[10,256,512]{1,2,0:T(8,128)(2,1)}), bf16[10,2048,512]{1,2,0:T(8,128)(2,1)}) %all-gather.4.cloned.1.call-update) | async-done | bytes 20971536 | tf_op jit(solution)/shard_map/all_gather | solution.py:82
  402.6 10.3 %convolution_bitcast_fusion = f32[10,256,512]{1,2,0:T(8,128)S(1)} fusion(bf16[10,2048,512]{1,2,0:T(8,128)(2,1)} %all-gather.4.cloned.1.call-done, bf16[256,2048]{1,0:T(8,128)(2,1)S(1)} %copy-done.20), kind=kOutput, calls=%fused_computation.38 | convolution fusion | flops 5368709120 | bytes 27262976 | tf_op jit(solution)/shard_map/jy,zyi->zji/dot_general | solution.py:79
  412.9 14.9 %fusion.62 = (bf16[10,256,512]{1,2,0:T(8,128)(2,1)}, bf16[1,256,512]{1,2,0:T(8,128)(2,1)S(1)}, f32[1,256,512]{1,2,0:T(8,128)S(1)}, f32[1,256,512]{1,2,0:T(8,128)...) fusion(f32[]{:T(128)S(6)} %neg.27, f32[]{:T(128)} %bitcast.4, ...), kind=kLoop, calls=%fused_computation.108 | loop fusion | flops 13631487 | bytes 8916080
  434.1 7.7 convert_dynamic-update-slice_fusion.5
  442.5 10.3 %convert_dynamic-update-slice_fusion.3 = bf16[10,256,512]{1,2,0:T(8,128)(2,1)} fusion(bf16[10,256,512]{1,2,0:T(8,128)(2,1)} %convert_dynamic-update-slice_fusion.4, f32[1,256,512]{1,2,0:T(8,128)S(1)} %get-tuple-element.7, f32[1,256,512]{1,2,0:T(8,128)S(1)} %get-tuple-element.6, f32[]{:T(128)} %bitcast.3, f32[]{:T(128)S(6)} %neg.27, f32[]{:T(128)} %bitcast.4, ...), kind=kLoop, calls=%fused_computation.112 | loop fusion | flops 5636096 | bytes 1320988
  453.5 14.0 %convert_dynamic-update-slice_fusion.1 = bf16[10,256,512]{1,2,0:T(8,128)(2,1)} fusion(bf16[10,256,512]{1,2,0:T(8,128)(2,1)} %convert_dynamic-update-slice_fusion.2, f32[]{:T(128)} %bitcast.3, f32[]{:T(128)S(6)} %neg.27, f32[]{:T(128)} %bitcast.4, f32[]{:T(128)} %bitcast.5, f32[]{:T(128)S(6)} %neg.28, f32[]{:T(128)} %bitcast.6, f32[]{:T(128)} %bitcast.7, ...), kind=kLoop, calls=%fused_computation.110 | loop fusion | flops 8912896 | bytes 2372132
  467.5 14.0 %convert_dynamic-update-slice_fusion = bf16[10,256,512]{1,2,0:T(8,128)(2,1)} fusion(bf16[10,256,512]{1,2,0:T(8,128)(2,1)} %convert_dynamic-update-slice_fusion.1, f32[]{:T(128)} %bitcast.3, f32[]{:T(128)S(6)} %neg.27, f32[]{:T(128)} %bitcast.4, f32[]{:T(128)} %bitcast.5, f32[]{:T(128)S(6)} %neg.28, f32[]{:T(128)} %bitcast.6, f32[]{:T(128)} %bitcast.7, ...), kind=kLoop, calls=%fused_computation.109 | loop fusion | flops 8650752 | bytes 2372132 | tf_op jit(solution)/shard_map/stack | solution.py:54
  481.7 184.6 %all-gather.6.cloned.1.call-done = bf16[10,2048,512]{1,2,0:T(8,128)(2,1)} async-done(((bf16[10,256,512]{1,2,0:T(8,128)(2,1)}), bf16[10,2048,512]{1,2,0:T(8,128)(2,1)}) %all-gather.6.cloned.1.call-update) | async-done | bytes 20971536 | tf_op jit(solution)/shard_map/all_gather | solution.py:95
  666.3 22.0 %convert_bitcast_fusion = bf16[10,256,512]{2,1,0:T(8,128)(2,1)} fusion(bf16[10,2048,512]{1,2,0:T(8,128)(2,1)} %all-gather.6.cloned.1.call-done, bf16[256,2048]{1,0:T(8,128)(2,1)S(1)} %copy-done.21), kind=kOutput, calls=%fused_computation.27 | convolution fusion | flops 5370019840 | bytes 24641536 | tf_op jit(solution)/shard_map/yj,zji->zyi/dot_general | solution.py:92
  689.0 9.1 select_bitcast_fusion
  698.2 10.4 %slice_convert_fusion.1 = (f32[1,10,256,512]{3,2,1,0:T(8,128)}, f32[1,10,256,512]{3,2,1,0:T(8,128)}) fusion(s32[2,10,256,512]{3,2,1,0:T(8,128)} %param.22), kind=kLoop, calls=%fused_computation.25 | loop fusion | flops 2621440 | bytes 20971520 | tf_op jit(solution)/shard_map/convert_element_type | solution.py:111
  708.6 82.6 %all-gather.8.cloned.1.call-done = bf16[10,256,2048]{2,1,0:T(8,128)(2,1)} async-done(((bf16[10,256,512]{2,1,0:T(8,128)(2,1)}), bf16[10,256,2048]{2,1,0:T(8,128)(2,1)}) %all-gather.8.cloned.1.call-update) | async-done | bytes 10485776 | tf_op jit(solution)/shard_map/all_gather | solution.py:101
  791.2 8.5 fusion.7
  799.8 5.9 pad_maximum_fusion.4
  826.5 5.4 collective-permute-start.5
  837.9 27.6 %pad_maximum_fusion = f32[4,10,258,514]{3,2,1,0:T(8,128)} fusion(f32[4,10,1,514]{3,2,1,0:T(1,128)S(1)} %collective-permute-done.6, f32[4,10,256,1]{3,2,1,0:T(8,128)S(1)} %copy-done.8, f32[1,10,256,512]{3,2,1,0:T(8,128)} %get-tuple-element.21, f32[1,10,256,512]{3,2,1,0:T(8,128)S(1)} %bitcast.56, f32[1,10,256,512]{3,2,1,0:T(8,128)} %select_bitcast_fusion, ...), kind=kLoop, calls=%fused_computation | loop fusion | flops 37131360 | bytes 42435840 | tf_op jit(solution)/shard_map/concatenate | solution.py:27
  865.5 18.5 %slice_bitcast_fusion.3 = (f32[10,258,514]{2,1,0:T(8,128)}, f32[10,258,514]{2,1,0:T(8,128)}, f32[10,258,514]{2,1,0:T(8,128)}, f32[10,258,514]{2,1,0:T(8,128)}) fusion(f32[4,10,258,514]{3,2,1,0:T(8,128)} %pad_maximum_fusion), kind=kLoop, calls=%fused_computation.6 | loop fusion | bytes 42435840 | tf_op jit(solution)/shard_map/squeeze | solution.py:118
  884.1 15.0 %fusion.3 = f32[10,256,513]{2,1,0:T(8,128)} fusion(f32[10,258,514]{2,1,0:T(8,128)} %get-tuple-element.16, f32[10,258,514]{2,1,0:T(8,128)} %get-tuple-element.17, f32[10,258,514]{2,1,0:T(8,128)} %get-tuple-element.14, pred[513]{0:T(1024)(128)(4,1)S(1)} %fusion.65), kind=kLoop, calls=%fused_computation.9 | loop fusion | flops 6566400 | bytes 31519232 | tf_op jit(solution)/shard_map/jit(_where)/select_n | solution.py:123
  900.9 10.7 %fusion.5 = f32[10,257,512]{2,1,0:T(8,128)} fusion(f32[10,258,514]{2,1,0:T(8,128)S(1)} %copy-done.2, f32[10,258,514]{2,1,0:T(8,128)S(1)} %copy-done.3, f32[10,258,514]{2,1,0:T(8,128)} %get-tuple-element.15, pred[257]{0:T(512)(128)(4,1)S(1)} %fusion.68), kind=kLoop, calls=%fused_computation.14 | loop fusion | flops 6579200 | bytes 31580416 | tf_op jit(solution)/shard_map/jit(_where)/select_n | solution.py:132
  911.7 11.2 %fusion.6 = f32[10,256,512]{2,1,0:T(8,128)} fusion(f32[10,257,512]{2,1,0:T(8,128)} %fusion.5, f32[10,256,513]{2,1,0:T(8,128)} %fusion.3), kind=kLoop, calls=%fused_computation.18 | loop fusion | flops 3932160 | bytes 26214400 | tf_op jit(solution)/shard_map/add | solution.py:134
  (88 shorter events, 67.6 us)
Async XLA Ops:
  7.2 194.8 %copy-start = (bf16[2048,512]{1,0:T(8,128)(2,1)S(1)}, bf16[2048,512]{1,0:T(8,128)(2,1)}, u32[]{:S(2)}) copy-start(bf16[2048,512]{1,0:T(8,128)(2,1)} %param.17) | copy-start | bytes 6291460
  7.2 395.4 %all-gather.4.cloned.1.call-start = ((), (), s32[]{:S(2)}) async-start(), calls=%async_computation | async-start | bytes 23592960 | tf_op jit(solution)/shard_map/all_gather | solution.py:82
  13.3 58.6 %collective-permute-start = (bf16[10,256,512]{2,1,0:T(8,128)(2,1)S(1)}, bf16[10,256,512]{2,1,0:T(8,128)(2,1)S(1)}, u32[]{:S(2)}, u32[]{:S(2)}) collective-permute-start(bf16[10,256,512]{2,1,0:T(8,128)(2,1)S(1)} %get-tuple-element.11), channel_id=1, source_target_pairs={{0,24},{8,0},{16,8},{24,16},{1,25},{9,1},{17,9},{25,17},{2,26},{10... | collective-permute-start | bytes 7864328 | tf_op jit(solution)/shard_map/ppermute | solution.py:12
  73.4 57.8 %collective-permute-start.1 = (bf16[10,256,512]{2,1,0:T(8,128)(2,1)S(1)}, bf16[10,256,512]{2,1,0:T(8,128)(2,1)}, u32[]{:S(2)}, u32[]{:S(2)}) collective-permute-start(bf16[10,256,512]{2,1,0:T(8,128)(2,1)S(1)} %collective-permute-done), channel_id=1, source_target_pairs={{0,24},{8,0},{16,8},{24,16},{1,25},{9,1},{17,9},{25,17},{2,26},{10... | collective-permute-start | bytes 7864328 | tf_op jit(solution)/shard_map/ppermute | solution.py:12
  131.2 57.1 %collective-permute-start.2 = (bf16[10,256,512]{2,1,0:T(8,128)(2,1)}, bf16[10,256,512]{2,1,0:T(8,128)(2,1)}, u32[]{:S(2)}, u32[]{:S(2)}) collective-permute-start(bf16[10,256,512]{2,1,0:T(8,128)(2,1)} %collective-permute-done.1), channel_id=1, source_target_pairs={{0,24},{8,0},{16,8},{24,16},{1,25},{9,1},{17,9},{25,17},{2,26},{10... | collective-permute-start | bytes 7864328 | tf_op jit(solution)/shard_map/ppermute | solution.py:12
  134.6 57.1 %copy-start.11 = (bf16[10,256,512]{2,1,0:T(8,128)(2,1)S(1)}, bf16[10,256,512]{2,1,0:T(8,128)(2,1)}, u32[]{:S(2)}) copy-start(bf16[10,256,512]{2,1,0:T(8,128)(2,1)} %copy-done.10) | copy-start | bytes 7864324
  138.2 55.2 %copy-start.13 = (bf16[10,256,512]{2,1,0:T(8,128)(2,1)S(1)}, bf16[10,256,512]{2,1,0:T(8,128)(2,1)}, u32[]{:S(2)}) copy-start(bf16[10,256,512]{2,1,0:T(8,128)(2,1)} %copy-done.12) | copy-start | bytes 7864324
  202.0 16.3 %copy-start.15 = (f32[10]{0:T(128)S(1)}, f32[10]{0:T(128)}, u32[]{:S(2)}) copy-start(f32[10]{0:T(128)} %param.16) | copy-start | bytes 124
  202.0 200.6 %copy-start.20 = (bf16[256,2048]{1,0:T(8,128)(2,1)S(1)}, bf16[256,2048]{1,0:T(8,128)(2,1)}, u32[]{:S(2)}) copy-start(bf16[256,2048]{1,0:T(8,128)(2,1)} %param.18) | copy-start | bytes 3145732
  211.6 454.7 %all-gather.6.cloned.1.call-start = ((), (), s32[]{:S(2)}) async-start(), calls=%async_computation.1 | async-start | bytes 23592960 | tf_op jit(solution)/shard_map/all_gather | solution.py:95
  219.0 193.8 %copy-start.14 = (f32[512]{0:T(512)S(1)}, f32[512]{0:T(512)}, u32[]{:S(2)}) copy-start(f32[512]{0:T(512)} %param.13) | copy-start | bytes 6148
  219.0 193.9 %copy-start.17 = (f32[256]{0:T(256)S(1)}, f32[256]{0:T(256)}, u32[]{:S(2)}) copy-start(f32[256]{0:T(256)} %param.14) | copy-start | bytes 3076
  441.7 224.5 %copy-start.21 = (bf16[256,2048]{1,0:T(8,128)(2,1)S(1)}, bf16[256,2048]{1,0:T(8,128)(2,1)}, u32[]{:S(2)}) copy-start(bf16[256,2048]{1,0:T(8,128)(2,1)} %param.19) | copy-start | bytes 3145732
  481.5 206.9 %copy-start.18 = (f32[4]{0:T(128)S(1)}, f32[4]{0:T(128)}, u32[]{:S(2)}) copy-start(f32[4]{0:T(128)} %param.23) | copy-start | bytes 52
  481.5 309.7 %all-gather.8.cloned.1.call-start = ((), (), s32[]{:S(2)}) async-start(), calls=%async_computation.2 | async-start | bytes 13107200 | tf_op jit(solution)/shard_map/all_gather | solution.py:101
  698.2 93.0 %copy-start.19 = (bf16[2048,512]{1,0:T(8,128)(2,1)S(1)}, bf16[2048,512]{1,0:T(8,128)(2,1)}, u32[]{:S(2)}) copy-start(bf16[2048,512]{1,0:T(8,128)(2,1)} %param.20) | copy-start | bytes 6291460
  809.0 8.6 collective-permute-start.3
  815.4 5.6 collective-permute-start.4
  821.1 16.8 %slice-start = ((s8[5242880]{0:T(1024)(128)(4,1)}), s8[1048576]{0:T(1024)(128)(4,1)S(1)}, s32[]{:S(2)}) async-start(s8[5242880]{0:T(1024)(128)(4,1)} %bitcast.55), calls=%async_computation.3 | async-start | bytes 2097152
  824.2 13.7 %copy-start.8 = (f32[4,10,256,1]{3,2,1,0:T(8,128)S(1)}, f32[4,10,256,1]{3,2,1,0:T(8,128)}, u32[]{:S(2)}) copy-start(f32[4,10,256,1]{3,2,1,0:T(8,128)} %copy.17) | copy-start | bytes 122884
  826.5 7.5 collective-permute-start.5
  831.9 6.0 collective-permute-start.6
  884.1 15.0 %copy-start.2 = (f32[10,258,514]{2,1,0:T(8,128)S(1)}, f32[10,258,514]{2,1,0:T(8,128)}, u32[]{:S(2)}) copy-start(f32[10,258,514]{2,1,0:T(8,128)} %get-tuple-element.16) | copy-start | bytes 15913444
  884.1 16.9 %copy-start.3 = (f32[10,258,514]{2,1,0:T(8,128)S(1)}, f32[10,258,514]{2,1,0:T(8,128)}, u32[]{:S(2)}) copy-start(f32[10,258,514]{2,1,0:T(8,128)} %get-tuple-element.17) | copy-start | bytes 15913444
  (10 other events, 83.3 us)
Sparse Core Ops, SparseCore 0:
  211.7 190.8 all-gather.3
  481.6 184.6 all-gather.5
  688.5 102.6 all-gather.7
